TPU v7x, 512 devices: a whole 4x8x8 slice. The times are simulated.
512 devices in a mesh: seq: 64 (over y, x, core), ch: 8 (over z).
Axes of the slice: x: 4, y: 8, z: 8, core: 2. Of those that a mesh axis runs over, the one named last changes fastest.
Arguments:
- signal: bfloat16 [1536, 32768], P('ch', 'seq'), may hold values from -16 to 16
- input_norm_gain: float32 [1536], P('ch'), may hold values from 0.25 to 1.75
- value_weight: bfloat16 [1536, 1536], P('seq', 'ch'), may hold values from -0.15625 to 0.15625
- gate_weight: bfloat16 [1536, 1536], P('seq', 'ch'), may hold values from -0.15625 to 0.15625
- depth_taps: float32 [31, 1536], P(None, 'ch'), may hold values from -1 to 1
- cotangent: bfloat16 [1536, 32768], P('ch', 'seq'), may hold values from -6 to 6
Outputs:
- output: bfloat16 [1536, 32768], P('ch', 'seq')
- signal_gradient: bfloat16 [1536, 32768], P('ch', 'seq')
- grad_value: float32 [1536, 1536], P('seq', 'ch')
- grad_gate: float32 [1536, 1536], P('seq', 'ch')
- grad_taps: float32 [31, 1536], P(None, 'ch')
- gain_gradient: float32 [1536], P('ch')
All inputs are finite; a program needn't handle non-finite values.
Results may differ from a plain program's by a relative error of at most 0.02.
Values may be sent and summed in bfloat16 or wider, within the bound.
No kernel may reach another device: no remote copies, remote signals or barrier semaphores. Data moves between devices by JAX's collectives and lax.ppermute only.
A program may use at most 64 MiB of HBM per device.

v0:
```python
import jax
import jax.numpy as jnp
from jax import lax
from jax.sharding import PartitionSpec as P


def extended(cells, sides, width):
    for axis, dim in sides:
        count = lax.axis_size(axis)
        ends = count - 1
        head = lax.slice_in_dim(cells, 0, width, axis=dim)
        tail = lax.slice_in_dim(cells, cells.shape[dim] - width, cells.shape[dim], axis=dim)
        cells = jnp.concatenate(
            [
                lax.ppermute(tail, axis, [(i, (i + 1) % count) for i in range(ends)]),
                cells,
                lax.ppermute(head, axis, [((i + 1) % count, i) for i in range(ends)]),
            ],
            axis=dim,
        )
    return cells


def standardize_rows(columns_in):
    values = columns_in.astype(jnp.float32)
    average = jnp.mean(values, 0, keepdims=True)
    centred = values - average
    spread = jnp.mean(centred * centred, 0, keepdims=True)
    inverse_deviation = lax.rsqrt(spread + 1e-05)
    return (centred * inverse_deviation, inverse_deviation)


def depthwise(padded, kernel):
    channels = padded.shape[0]
    result = lax.conv_general_dilated(
        padded[None],
        kernel,
        (1,),
        "VALID",
        dimension_numbers=("NCH", "OIH", "NCH"),
        feature_group_count=channels,
        precision=lax.Precision.HIGHEST,
    )
    return result[0]


def shards(signal, input_norm_gain, value_weight, gate_weight, depth_taps, cotangent):
    local_cols = signal.shape[0]
    seq_position = lax.axis_index("seq")
    channel_position = lax.axis_index("ch")
    reach = depth_taps.shape[0] // 2
    complete_signal = lax.all_gather(signal, "ch", axis=0, tiled=True)
    complete_gain = lax.all_gather(input_norm_gain, "ch", axis=0, tiled=True)
    centered_unit, inverse_deviation = standardize_rows(complete_signal)
    normalized_signal = (centered_unit * complete_gain[:, None]).astype(jnp.bfloat16)
    centered_unit_rows = lax.dynamic_slice_in_dim(
        centered_unit, channel_position * local_cols, local_cols, 0
    )
    stacked = jnp.concatenate([value_weight, gate_weight], 1)
    gathered = lax.all_gather(stacked, "seq", axis=0, tiled=True)
    mixed = lax.dot_general(
        gathered, normalized_signal, (((0,), (0,)), ((), ())), preferred_element_type=jnp.float32
    )
    value = mixed[:local_cols]
    gate = mixed[local_cols:]
    sig_gate = jax.nn.sigmoid(gate)
    glued = (value * sig_gate).astype(jnp.bfloat16)
    glued_pad = extended(glued, (("seq", 1),), reach).astype(jnp.float32)
    forward_kernel = depth_taps.T[:, None, :]
    pre = depthwise(glued_pad, forward_kernel)
    sig_pre = jax.nn.sigmoid(pre)
    output = (pre * sig_pre).astype(jnp.bfloat16)
    grad_pre = (cotangent.astype(jnp.float32) * sig_pre * (1.0 + pre * (1.0 - sig_pre))).astype(
        jnp.bfloat16
    )
    grad_pre_f = grad_pre.astype(jnp.float32)
    grad_pad = extended(grad_pre, (("seq", 1),), reach).astype(jnp.float32)
    grad_glued = depthwise(grad_pad, forward_kernel[:, :, ::-1])
    tap_partial = depthwise(glued_pad, grad_pre_f[:, None, :]).T
    grad_v = (grad_glued * sig_gate).astype(jnp.bfloat16)
    grad_g = (grad_glued * value * sig_gate * (1.0 - sig_gate)).astype(jnp.bfloat16)
    grad_both = jnp.concatenate([grad_v, grad_g], 0)
    weight_partial = lax.dot_general(
        normalized_signal, grad_both, (((1,), (1,)), ((), ())), preferred_element_type=jnp.float32
    )
    normed_term = jnp.dot(gathered, grad_both, preferred_element_type=jnp.float32)
    normalized_gradient = lax.psum_scatter(
        normed_term.astype(jnp.bfloat16), "ch", scatter_dimension=0, tiled=True
    ).astype(jnp.float32)
    scaled_signal = normalized_gradient * input_norm_gain[:, None]
    moments = jnp.concatenate(
        [
            jnp.sum(scaled_signal, 0, keepdims=True),
            jnp.sum(scaled_signal * centered_unit_rows, 0, keepdims=True),
        ],
        0,
    )
    moments = lax.psum(moments, "ch") * (1.0 / complete_signal.shape[0])
    inverse_rows = inverse_deviation
    signal_gradient = (
        inverse_rows * (scaled_signal - moments[0:1] - centered_unit_rows * moments[1:2])
    ).astype(jnp.bfloat16)
    gain_portion = jnp.sum(normalized_gradient * centered_unit_rows, 1)
    extra = jnp.concatenate([tap_partial, gain_portion[None]], 0)
    extra = jnp.pad(extra, ((0, 0), (0, weight_partial.shape[1] - extra.shape[1])))
    summed = lax.psum(jnp.concatenate([weight_partial, extra], 0), "seq")
    rows = value_weight.shape[0]
    weight_sums = lax.dynamic_slice_in_dim(summed, seq_position * rows, rows, 0)
    grad_value = weight_sums[:, :local_cols]
    grad_gate = weight_sums[:, local_cols:]
    taps_rows = depth_taps.shape[0]
    full_rows = weight_partial.shape[0]
    grad_taps = summed[full_rows : full_rows + taps_rows, :local_cols]
    gain_gradient = summed[full_rows + taps_rows, :local_cols]
    return (output, signal_gradient, grad_value, grad_gate, grad_taps, gain_gradient)


def solution(mesh):
    placed = (
        P("ch", "seq"),
        P("ch"),
        P("seq", "ch"),
        P("seq", "ch"),
        P(None, "ch"),
        P("ch", "seq"),
    )
    return jax.shard_map(
        shards,
        mesh=mesh,
        in_specs=placed,
        out_specs=(
            P("ch", "seq"),
            P("ch", "seq"),
            P("seq", "ch"),
            P("seq", "ch"),
            P(None, "ch"),
            P("ch"),
        ),
        check_vma=False,
    )
```

profile of v0, /device:TPU:25, one launch (start us, length us, event | category | flops | bytes accessed | tf_op | source)
XLA Modules:
  0.0 444.6 jit_solution(922992032706214905)
XLA Ops:
  8.0 1.4 pad_maximum_fusion.5
  9.5 1.3 dynamic-slice
  12.3 19.7 %all-reduce.1 = f32[1536]{0:T(1024)S(1)} all-reduce(f32[1536]{0:T(1024)S(1)} %dynamic-update-slice), channel_id=1, replica_groups=mesh['seq'=64,'ch'=8] {'ch'}, use_global_device_ids=true, to_apply=%add.1 | all-reduce | flops 1536 | bytes 12288
  32.0 22.1 %all-gather.5.cloned.1.call-done = bf16[1536,512]{1,0:T(8,128)(2,1)} async-done(((bf16[192,512]{1,0:T(8,128)(2,1)}), bf16[1536,512]{1,0:T(8,128)(2,1)}) %all-gather.5.cloned.1.call-update) | async-done | bytes 1572880 | tf_op jit(solution)/shard_map/all_gather | solution.py:52
  54.1 1.8 convert_reduce_fusion
  56.5 84.5 %all-gather.3.cloned.1.call-done = bf16[1536,384]{1,0:T(8,128)(2,1)} async-done(((bf16[24,384]{1,0:T(8,128)(2,1)}), bf16[1536,384]{1,0:T(8,128)(2,1)}) %all-gather.3.cloned.1.call-update) | async-done | bytes 1179664 | tf_op jit(solution)/shard_map/all_gather | solution.py:60
  141.0 2.1 fusion.29
  143.4 2.2 collective-permute-start.1
  145.5 3.4 collective-permute-start
  149.0 1.1 collective-permute-done
  151.9 2.0 convolution_select_fusion.1
  153.9 1.4 copy.36
  156.3 2.0 multiply_convert_fusion.3
  158.4 6.4 %collective-permute-start.3 = (bf16[192,15]{1,0:T(8,128)(2,1)S(1)}, bf16[192,15]{1,0:T(8,128)(2,1)S(1)}, u32[]{:S(2)}, u32[]{:S(2)}) collective-permute-start(bf16[192,15]{1,0:T(8,128)(2,1)S(1)} %get-tuple-element.18), channel_id=1, source_target_pairs={{8,0},{16,8},{24,16},{32,24},{40,32},{48,40},{56,48},{64,56},{72,6... | collective-permute-start | bytes 17288 | tf_op jit(solution)/shard_map/ppermute | solution.py:17
  164.8 1.9 collective-permute-start.2
  166.8 1.2 collective-permute-done.2
  169.0 2.0 convolution_select_fusion
  171.0 1.4 copy.37
  173.5 1.2 multiply_convert_fusion.2
  174.6 3.4 convolution_convert_fusion
  178.3 2.1 fusion
  181.7 2.2 fusion.48
  184.0 2.4 fusion.28
  186.4 37.6 %reduce-scatter.2.cloned.1.call-done = bf16[192,512]{1,0:T(8,128)(2,1)} async-done(((bf16[1536,512]{1,0:T(8,128)(2,1)}), bf16[192,512]{1,0:T(8,128)(2,1)}) %reduce-scatter.2.cloned.1.call-update) | async-done | bytes 196624 | tf_op jit(solution)/shard_map/reduce_scatter | solution.py:87
  224.0 1.3 fusion.24
  225.3 3.3 pad_maximum_fusion
  228.6 12.6 %psum.14 = f32[2,512]{1,0:T(2,128)S(1)} all-reduce(f32[2,512]{1,0:T(2,128)S(1)} %pad_maximum_fusion.6), channel_id=1, replica_groups=mesh['seq'=64,'ch'=8] {'ch'}, use_global_device_ids=true, to_apply=%region_5.0 | all-reduce | flops 1024 | bytes 8192 | tf_op jit(solution)/shard_map/psum | solution.py:98
  241.2 1.8 fusion.23
  243.0 190.9 %all-reduce.4.cloned.1.call-done = f32[1568,384]{1,0:T(8,128)} async-done(((f32[1568,384]{1,0:T(8,128)}), f32[1568,384]{1,0:T(8,128)}) %all-reduce.4.cloned.1.call-update) | async-done | bytes 2408464 | tf_op jit(solution)/shard_map/psum | solution.py:106
  433.9 1.4 slice.64
  435.3 1.3 slice.65
  436.5 1.5 fusion.44
  (49 shorter events, 9.0 us)
Async XLA Ops:
  7.2 144.7 %copy-start = (f32[31,192]{1,0:T(8,128)S(1)}, f32[31,192]{1,0:T(8,128)}, u32[]{:S(2)}) copy-start(f32[31,192]{1,0:T(8,128)} %param.10) | copy-start | bytes 71428
  7.2 46.9 %all-gather.5.cloned.1.call-start = ((), (), s32[]{:S(2)}) async-start(), calls=%async_computation.2 | async-start | bytes 1769472 | tf_op jit(solution)/shard_map/all_gather | solution.py:52
  7.9 133.1 %all-gather.3.cloned.1.call-start = ((), (), s32[]{:S(2)}) async-start(), calls=%async_computation.1 | async-start | bytes 1198080 | tf_op jit(solution)/shard_map/all_gather | solution.py:60
  9.4 214.6 %reduce-scatter.2.cloned.1.call-start = ((), (), s32[]{:S(2)}) async-start(), calls=%async_computation.3 | async-start | bytes 1769472 | tf_op jit(solution)/shard_map/reduce_scatter | solution.py:87
  54.1 1.9 copy-start.1
  143.2 8.7 %copy-start.5 = (pred[8,68]{0,1:T(8,128)(4,1)S(1)}, pred[8,68]{0,1:T(8,128)(4,1)}, u32[]{:S(2)}) copy-start(pred[8,68]{0,1:T(8,128)(4,1)} %constant.49) | copy-start | bytes 1636
  143.4 5.6 %collective-permute-start.1 = (bf16[192,15]{1,0:T(8,128)(2,1)S(1)}, bf16[192,15]{1,0:T(8,128)(2,1)S(1)}, u32[]{:S(2)}, u32[]{:S(2)}) collective-permute-start(bf16[192,15]{1,0:T(8,128)(2,1)S(1)} %get-tuple-element.20), channel_id=1, source_target_pairs={{8,0},{16,8},{24,16},{32,24},{40,32},{48,40},{56,48},{64,56},{72,6... | collective-permute-start | bytes 17288 | tf_op jit(solution)/shard_map/ppermute | solution.py:17
  145.5 4.6 %collective-permute-start = (bf16[192,15]{1,0:T(8,128)(2,1)S(1)}, bf16[192,15]{1,0:T(8,128)(2,1)S(1)}, u32[]{:S(2)}, u32[]{:S(2)}) collective-permute-start(bf16[192,15]{1,0:T(8,128)(2,1)S(1)} %get-tuple-element.19), channel_id=1, source_target_pairs={{0,8},{8,16},{16,24},{24,32},{32,40},{40,48},{48,56},{56,64},{64,7... | collective-permute-start | bytes 17288 | tf_op jit(solution)/shard_map/ppermute | solution.py:15
  158.4 8.4 %collective-permute-start.3 = (bf16[192,15]{1,0:T(8,128)(2,1)S(1)}, bf16[192,15]{1,0:T(8,128)(2,1)S(1)}, u32[]{:S(2)}, u32[]{:S(2)}) collective-permute-start(bf16[192,15]{1,0:T(8,128)(2,1)S(1)} %get-tuple-element.18), channel_id=1, source_target_pairs={{8,0},{16,8},{24,16},{32,24},{40,32},{48,40},{56,48},{64,56},{72,6... | collective-permute-start | bytes 17288 | tf_op jit(solution)/shard_map/ppermute | solution.py:17
  164.8 3.1 collective-permute-start.2
  178.0 2.4 copy-start.2
  178.1 255.9 %all-reduce.4.cloned.1.call-start = ((), (), s32[]{:S(2)}) async-start(), calls=%async_computation.4 | async-start | bytes 4816896 | tf_op jit(solution)/shard_map/psum | solution.py:106
  184.0 40.0 %copy-start.4 = (f32[192]{0:T(256)S(1)}, f32[192]{0:T(256)}, u32[]{:S(2)}) copy-start(f32[192]{0:T(256)} %param.7) | copy-start | bytes 2308
  228.6 12.6 %copy-start.3 = (bf16[192,512]{1,0:T(8,128)(2,1)S(1)}, bf16[192,512]{1,0:T(8,128)(2,1)}, u32[]{:S(2)}) copy-start(bf16[192,512]{1,0:T(8,128)(2,1)} %reduce-scatter.2.cloned.1.call-done) | copy-start | bytes 589828
Sparse Core Ops, SparseCore 0:
  10.1 43.9 all-gather.4
  57.9 83.0 all-gather.2
  178.2 45.7 reduce-scatter.1
  228.7 205.1 all-reduce.3
where the time goes:
time: 445 us
  waiting for transfers between devices  338 us (76%)
  blocking collectives  32.2 us (7%)
  other arithmetic  16.4 us (4%)
  between operations  14.7 us (3%)
  local copies, waits for them, and re-layouts  14.5 us (3%)
  starting transfers between devices  14.3 us (3%)
  matrix products  14.2 us (3%)
    psum x1, waiting for transfers between devices, shards(): summed = lax.psum(jnp.concatenate([weight_partial, extra], 0), 'seq')  191 us
    all_gather x1, waiting for transfers between devices, shards(): gathered = lax.all_gather(stacked, 'seq', axis=0, tiled=True)  84.5 us
    reduce_scatter x1, waiting for transfers between devices, shards(): lax.psum_scatter(normed_term.astype(jnp.bfloat16), 'ch', scatter_dimensio...  37.6 us
    all_gather x1, waiting for transfers between devices, shards(): complete_signal = lax.all_gather(signal, 'ch', axis=0, tiled=True)  22.1 us
    unnamed x1, blocking collectives  19.7 us
    psum x1, blocking collectives, shards(): moments = lax.psum(moments, 'ch') * (1.0 / complete_signal.shape[0])  12.6 us
  transfers between devices with their start and end apart: 8, of which 6 were waited for; matrix products, arithmetic and copies ran while one was open for 4% of the time, Pallas kernels for 0%

commit v1 on v0

--- a/solution.py
+++ b/solution.py
@@ -2,6 +2,12 @@
 import jax.numpy as jnp
 from jax import lax
 from jax.sharding import PartitionSpec as P
+
+
+def joined_along(pieces, dim):
+    dims = list(pieces.shape[1:])
+    dims[dim] *= pieces.shape[0]
+    return jnp.moveaxis(pieces, 0, dim).reshape(dims)
 
 
 def extended(cells, sides, width):
@@ -49,7 +55,19 @@
     seq_position = lax.axis_index("seq")
     channel_position = lax.axis_index("ch")
     reach = depth_taps.shape[0] // 2
-    complete_signal = lax.all_gather(signal, "ch", axis=0, tiled=True)
+    devices = lax.axis_size("ch")
+    pairs = [(i_2, (i_2 + 1) % devices) for i_2 in range(devices)]
+    back = [(b, a) for a, b in pairs]
+    lower, upper = ([], [])
+    for step in range(devices - 1):
+        if step % 2 == 0:
+            lower.append(lax.ppermute(lower[-1] if lower else signal, "ch", pairs))
+        else:
+            upper.append(lax.ppermute(upper[-1] if upper else signal, "ch", back))
+    blocks = jnp.stack([*lower[::-1], signal, *upper])
+    shift = lax.axis_index("ch") - len(lower)
+    blocks = blocks[(jnp.arange(devices) - shift) % devices]
+    complete_signal = joined_along(blocks, 0)
     complete_gain = lax.all_gather(input_norm_gain, "ch", axis=0, tiled=True)
     centered_unit, inverse_deviation = standardize_rows(complete_signal)
     normalized_signal = (centered_unit * complete_gain[:, None]).astype(jnp.bfloat16)

time: 445 us -> 419 us (0.942)
  waiting for transfers between devices: 338 us -> 298 us
  starting transfers between devices: 14.3 us -> 34.7 us
  blocking collectives: 32.2 us -> 26.1 us
    all_gather x1, waiting for transfers between devices: 84.5 us -> 45.6 us  [shards(): gathered = lax.all_gather(stacked, 'seq', axis=0, tiled=True)]
    all_gather x1 -> x0, waiting for transfers between devices: 22.1 us -> none  [shards(): complete_signal = lax.all_gather(signal, 'ch', axis=0, tiled=True)]
    ppermute x0 -> x7, starting transfers between devices: none -> 20.5 us  [the longest x4 11.3 us: shards(): lower.append(lax.ppermute(lower[-1] if lower else signal, 'ch', pairs))]
    ppermute x0 -> x7, waiting for transfers between devices: none -> 20.5 us  [the longest x4 13.3 us: shards(): lower.append(lax.ppermute(lower[-1] if lower else signal, 'ch', pairs))]
    unnamed x1, blocking collectives: 19.7 us -> 13.6 us
  transfers between devices with their start and end apart: 8 -> 14, of which waited for: 6 -> 9; matrix products, arithmetic and copies ran while one was open for 4% -> 4% of each run, Pallas kernels for 0% -> 0%
where the time goes in v1:
time: 419 us; the launch traced here: 418 us
  waiting for transfers between devices  298 us (71%)
  starting transfers between devices  34.7 us (8%)
  blocking collectives  26.1 us (6%)
  local copies, waits for them, and re-layouts  16.1 us (4%)
  other arithmetic  15.1 us (4%)
  between operations  14.8 us (4%)
  matrix products  12.9 us (3%)
    psum x1, waiting for transfers between devices, shards(): summed = lax.psum(jnp.concatenate([weight_partial, extra], 0), 'seq')  191 us
    all_gather x1, waiting for transfers between devices, shards(): gathered = lax.all_gather(stacked, 'seq', axis=0, tiled=True)  45.6 us
    reduce_scatter x1, waiting for transfers between devices, shards(): lax.psum_scatter(normed_term.astype(jnp.bfloat16), 'ch', scatter_dimensio...  39.1 us
    unnamed x1, blocking collectives  13.6 us
    ppermute x4, waiting for transfers between devices, shards(): lower.append(lax.ppermute(lower[-1] if lower else signal, 'ch', pairs))  13.3 us
    psum x1, blocking collectives, shards(): moments = lax.psum(moments, 'ch') * (1.0 / complete_signal.shape[0])  12.5 us
    ppermute x4, starting transfers between devices, shards(): lower.append(lax.ppermute(lower[-1] if lower else signal, 'ch', pairs))  11.3 us
    ppermute x3, starting transfers between devices, shards(): upper.append(lax.ppermute(upper[-1] if upper else signal, 'ch', back))  9.21 us
  transfers between devices with their start and end apart: 14, of which 9 were waited for; matrix products, arithmetic and copies ran while one was open for 4% of the time, Pallas kernels for 0%

profile of v1, /device:TPU:25, one launch (start us, length us, event | category | flops | bytes accessed | tf_op | source)
XLA Modules:
  0.0 418.2 jit_solution(9046530505331104461)
XLA Ops:
  7.2 4.1 collective-permute-start
  11.4 11.5 %collective-permute-done = bf16[192,512]{1,0:T(8,128)(2,1)S(1)} collective-permute-done((bf16[192,512]{1,0:T(8,128)(2,1)}, bf16[192,512]{1,0:T(8,128)(2,1)S(1)}, u32[]{:S(2)}, u32[]{:S(2)}) %collective-permute-start) | collective-permute-done | bytes 196640 | tf_op jit(solution)/shard_map/ppermute | solution.py:64
  22.9 1.9 collective-permute-start.1
  24.8 4.6 %collective-permute-start.4 = (bf16[192,512]{1,0:T(8,128)(2,1)}, bf16[192,512]{1,0:T(8,128)(2,1)S(1)}, u32[]{:S(2)}, u32[]{:S(2)}) collective-permute-start(bf16[192,512]{1,0:T(8,128)(2,1)} %param.6), channel_id=1, source_target_pairs={{1,0},{2,1},{3,2},{4,3},{5,4},{6,5},{7,6},{0,7},{9,8},{10,9},{11,1... | collective-permute-start | bytes 589832 | tf_op jit(solution)/shard_map/ppermute | solution.py:66
  29.4 1.8 collective-permute-done.1
  31.1 1.9 collective-permute-start.2
  37.4 13.6 %all-reduce.1 = f32[1536]{0:T(1024)S(1)} all-reduce(f32[1536]{0:T(1024)S(1)} %dynamic-update-slice), channel_id=1, replica_groups=mesh['seq'=64,'ch'=8] {'ch'}, use_global_device_ids=true, to_apply=%add.1 | all-reduce | flops 1536 | bytes 12288
  51.0 1.9 collective-permute-start.5
  53.0 3.4 collective-permute-start.3
  56.4 1.5 collective-permute-done.5
  57.8 2.7 collective-permute-start.6
  60.8 5.8 %collective-permute-done.6 = bf16[192,512]{1,0:T(8,128)(2,1)S(1)} collective-permute-done((bf16[192,512]{1,0:T(8,128)(2,1)S(1)}, bf16[192,512]{1,0:T(8,128)(2,1)S(1)}, u32[]{:S(2)}, u32[]{:S(2)}) %collective-permute-start.6) | collective-permute-done | bytes 196640 | tf_op jit(solution)/shard_map/ppermute | solution.py:66
  68.0 2.1 fusion
  70.1 45.6 %all-gather.2.cloned.1.call-done = bf16[1536,384]{1,0:T(8,128)(2,1)} async-done(((bf16[24,384]{1,0:T(8,128)(2,1)}), bf16[1536,384]{1,0:T(8,128)(2,1)}) %all-gather.2.cloned.1.call-update) | async-done | bytes 1179664 | tf_op jit(solution)/shard_map/all_gather | solution.py:78
  115.7 2.1 fusion.48
  118.0 2.2 collective-permute-start.8
  120.2 3.4 collective-permute-start.7
  126.5 2.0 convolution_select_fusion.1
  131.0 2.0 multiply_convert_fusion.3
  133.0 6.4 %collective-permute-start.10 = (bf16[192,15]{1,0:T(8,128)(2,1)S(1)}, bf16[192,15]{1,0:T(8,128)(2,1)S(1)}, u32[]{:S(2)}, u32[]{:S(2)}) collective-permute-start(bf16[192,15]{1,0:T(8,128)(2,1)S(1)} %get-tuple-element.20), channel_id=1, source_target_pairs={{8,0},{16,8},{24,16},{32,24},{40,32},{48,40},{56,48},{64,56},{72,6... | collective-permute-start | bytes 17288 | tf_op jit(solution)/shard_map/ppermute | solution.py:23
  139.5 1.9 collective-permute-start.9
  143.6 2.0 convolution_select_fusion
  145.7 1.4 copy.37
  149.5 2.1 convolution_convert_fusion
  153.9 2.2 fusion.47
  156.2 2.4 fusion.26
  158.6 39.1 %reduce-scatter.2.cloned.1.call-done = bf16[192,512]{1,0:T(8,128)(2,1)} async-done(((bf16[1536,512]{1,0:T(8,128)(2,1)}), bf16[192,512]{1,0:T(8,128)(2,1)}) %reduce-scatter.2.cloned.1.call-update) | async-done | bytes 196624 | tf_op jit(solution)/shard_map/reduce_scatter | solution.py:105
  198.9 3.3 pad_maximum_fusion
  202.3 12.5 %psum.14 = f32[2,512]{1,0:T(2,128)S(1)} all-reduce(f32[2,512]{1,0:T(2,128)S(1)} %pad_maximum_fusion.6), channel_id=1, replica_groups=mesh['seq'=64,'ch'=8] {'ch'}, use_global_device_ids=true, to_apply=%region_5.6 | all-reduce | flops 1024 | bytes 8192 | tf_op jit(solution)/shard_map/psum | solution.py:116
  214.8 1.8 fusion.21
  216.6 190.9 %all-reduce.4.cloned.1.call-done = f32[1568,384]{1,0:T(8,128)} async-done(((f32[1568,384]{1,0:T(8,128)}), f32[1568,384]{1,0:T(8,128)}) %all-reduce.4.cloned.1.call-update) | async-done | bytes 2408464 | tf_op jit(solution)/shard_map/psum | solution.py:124
  410.2 1.5 fusion.43
  (73 shorter events, 21.7 us)
Async XLA Ops:
  7.2 119.3 %copy-start = (f32[31,192]{1,0:T(8,128)S(1)}, f32[31,192]{1,0:T(8,128)}, u32[]{:S(2)}) copy-start(f32[31,192]{1,0:T(8,128)} %param.10) | copy-start | bytes 71428
  7.2 53.5 %copy-start.4 = (bf16[192,512]{1,0:T(8,128)(2,1)S(1)}, bf16[192,512]{1,0:T(8,128)(2,1)}, u32[]{:S(2)}) copy-start(bf16[192,512]{1,0:T(8,128)(2,1)} %param.6) | copy-start | bytes 589828
  7.2 108.5 %all-gather.2.cloned.1.call-start = ((), (), s32[]{:S(2)}) async-start(), calls=%async_computation.1 | async-start | bytes 1198080 | tf_op jit(solution)/shard_map/all_gather | solution.py:78
  7.2 15.6 %collective-permute-start = (bf16[192,512]{1,0:T(8,128)(2,1)}, bf16[192,512]{1,0:T(8,128)(2,1)S(1)}, u32[]{:S(2)}, u32[]{:S(2)}) collective-permute-start(bf16[192,512]{1,0:T(8,128)(2,1)} %param.6), channel_id=1, source_target_pairs={{0,1},{1,2},{2,3},{3,4},{4,5},{5,6},{6,7},{7,0},{8,9},{9,10},{10,1... | collective-permute-start | bytes 589832 | tf_op jit(solution)/shard_map/ppermute | solution.py:64
  22.9 8.3 %collective-permute-start.1 = (bf16[192,512]{1,0:T(8,128)(2,1)S(1)}, bf16[192,512]{1,0:T(8,128)(2,1)S(1)}, u32[]{:S(2)}, u32[]{:S(2)}) collective-permute-start(bf16[192,512]{1,0:T(8,128)(2,1)S(1)} %collective-permute-done), channel_id=1, source_target_pairs={{0,1},{1,2},{2,3},{3,4},{4,5},{5,6},{6,7},{7,0},{8,9},{9,10},{10,1... | collective-permute-start | bytes 589832 | tf_op jit(solution)/shard_map/ppermute | solution.py:64
  24.8 26.2 %collective-permute-start.4 = (bf16[192,512]{1,0:T(8,128)(2,1)}, bf16[192,512]{1,0:T(8,128)(2,1)S(1)}, u32[]{:S(2)}, u32[]{:S(2)}) collective-permute-start(bf16[192,512]{1,0:T(8,128)(2,1)} %param.6), channel_id=1, source_target_pairs={{1,0},{2,1},{3,2},{4,3},{5,4},{6,5},{7,6},{0,7},{9,8},{10,9},{11,1... | collective-permute-start | bytes 589832 | tf_op jit(solution)/shard_map/ppermute | solution.py:66
  31.1 21.8 %collective-permute-start.2 = (bf16[192,512]{1,0:T(8,128)(2,1)S(1)}, bf16[192,512]{1,0:T(8,128)(2,1)S(1)}, u32[]{:S(2)}, u32[]{:S(2)}) collective-permute-start(bf16[192,512]{1,0:T(8,128)(2,1)S(1)} %collective-permute-done.1), channel_id=1, source_target_pairs={{0,1},{1,2},{2,3},{3,4},{4,5},{5,6},{6,7},{7,0},{8,9},{9,10},{10,1... | collective-permute-start | bytes 589832 | tf_op jit(solution)/shard_map/ppermute | solution.py:64
  34.5 163.2 %reduce-scatter.2.cloned.1.call-start = ((), (), s32[]{:S(2)}) async-start(), calls=%async_computation.2 | async-start | bytes 1769472 | tf_op jit(solution)/shard_map/reduce_scatter | solution.py:105
  51.0 6.8 %collective-permute-start.5 = (bf16[192,512]{1,0:T(8,128)(2,1)S(1)}, bf16[192,512]{1,0:T(8,128)(2,1)S(1)}, u32[]{:S(2)}, u32[]{:S(2)}) collective-permute-start(bf16[192,512]{1,0:T(8,128)(2,1)S(1)} %collective-permute-done.4), channel_id=1, source_target_pairs={{1,0},{2,1},{3,2},{4,3},{5,4},{6,5},{7,6},{0,7},{9,8},{10,9},{11,1... | collective-permute-start | bytes 589832 | tf_op jit(solution)/shard_map/ppermute | solution.py:66
  53.0 7.6 %collective-permute-start.3 = (bf16[192,512]{1,0:T(8,128)(2,1)S(1)}, bf16[192,512]{1,0:T(8,128)(2,1)S(1)}, u32[]{:S(2)}, u32[]{:S(2)}) collective-permute-start(bf16[192,512]{1,0:T(8,128)(2,1)S(1)} %collective-permute-done.2), channel_id=1, source_target_pairs={{0,1},{1,2},{2,3},{3,4},{4,5},{5,6},{6,7},{7,0},{8,9},{9,10},{10,1... | collective-permute-start | bytes 589832 | tf_op jit(solution)/shard_map/ppermute | solution.py:64
  57.8 8.7 %collective-permute-start.6 = (bf16[192,512]{1,0:T(8,128)(2,1)S(1)}, bf16[192,512]{1,0:T(8,128)(2,1)S(1)}, u32[]{:S(2)}, u32[]{:S(2)}) collective-permute-start(bf16[192,512]{1,0:T(8,128)(2,1)S(1)} %collective-permute-done.5), channel_id=1, source_target_pairs={{1,0},{2,1},{3,2},{4,3},{5,4},{6,5},{7,6},{0,7},{9,8},{10,9},{11,1... | collective-permute-start | bytes 589832 | tf_op jit(solution)/shard_map/ppermute | solution.py:66
  117.9 8.6 %copy-start.6 = (pred[8,68]{0,1:T(8,128)(4,1)S(1)}, pred[8,68]{0,1:T(8,128)(4,1)}, u32[]{:S(2)}) copy-start(pred[8,68]{0,1:T(8,128)(4,1)} %constant.68) | copy-start | bytes 1636
  118.0 5.6 %collective-permute-start.8 = (bf16[192,15]{1,0:T(8,128)(2,1)S(1)}, bf16[192,15]{1,0:T(8,128)(2,1)S(1)}, u32[]{:S(2)}, u32[]{:S(2)}) collective-permute-start(bf16[192,15]{1,0:T(8,128)(2,1)S(1)} %get-tuple-element.22), channel_id=1, source_target_pairs={{8,0},{16,8},{24,16},{32,24},{40,32},{48,40},{56,48},{64,56},{72,6... | collective-permute-start | bytes 17288 | tf_op jit(solution)/shard_map/ppermute | solution.py:23
  120.2 4.6 %collective-permute-start.7 = (bf16[192,15]{1,0:T(8,128)(2,1)S(1)}, bf16[192,15]{1,0:T(8,128)(2,1)S(1)}, u32[]{:S(2)}, u32[]{:S(2)}) collective-permute-start(bf16[192,15]{1,0:T(8,128)(2,1)S(1)} %get-tuple-element.21), channel_id=1, source_target_pairs={{0,8},{8,16},{16,24},{24,32},{32,40},{40,48},{48,56},{56,64},{64,7... | collective-permute-start | bytes 17288 | tf_op jit(solution)/shard_map/ppermute | solution.py:21
  133.0 8.4 %collective-permute-start.10 = (bf16[192,15]{1,0:T(8,128)(2,1)S(1)}, bf16[192,15]{1,0:T(8,128)(2,1)S(1)}, u32[]{:S(2)}, u32[]{:S(2)}) collective-permute-start(bf16[192,15]{1,0:T(8,128)(2,1)S(1)} %get-tuple-element.20), channel_id=1, source_target_pairs={{8,0},{16,8},{24,16},{32,24},{40,32},{48,40},{56,48},{64,56},{72,6... | collective-permute-start | bytes 17288 | tf_op jit(solution)/shard_map/ppermute | solution.py:23
  139.5 3.1 collective-permute-start.9
  148.1 1.4 copy-start.1
  151.7 0.9 copy-start.2
  151.7 255.8 %all-reduce.4.cloned.1.call-start = ((), (), s32[]{:S(2)}) async-start(), calls=%async_computation.3 | async-start | bytes 4816896 | tf_op jit(solution)/shard_map/psum | solution.py:124
  156.2 41.5 %copy-start.5 = (f32[192]{0:T(256)S(1)}, f32[192]{0:T(256)}, u32[]{:S(2)}) copy-start(f32[192]{0:T(256)} %param.7) | copy-start | bytes 2308
  202.3 12.6 %copy-start.3 = (bf16[192,512]{1,0:T(8,128)(2,1)S(1)}, bf16[192,512]{1,0:T(8,128)(2,1)}, u32[]{:S(2)}) copy-start(bf16[192,512]{1,0:T(8,128)(2,1)} %reduce-scatter.2.cloned.1.call-done) | copy-start | bytes 589828
Sparse Core Ops, SparseCore 0:
  34.6 81.0 all-gather.1
  151.8 45.7 reduce-scatter.1
  202.4 205.0 all-reduce.3
